TPU v7x, 256 devices: a whole 4x4x8 slice. The times are simulated.
256 devices in a mesh: ctx: 64 (over z, y_hi, x), tp: 4 (over y_lo, core).
Axes of the slice: x: 4, y: 4 (y_hi: 2, y_lo: 2; y = y_hi * 2 + y_lo), z: 8, core: 2. Of those that a mesh axis runs over, the one named last changes fastest.
Arguments:
- query_in: bfloat16 [2048, 8192], P('tp', 'ctx'), may hold values from -6 to 6
- key_in: bfloat16 [2048, 8192], P('tp', 'ctx'), may hold values from -6 to 6
- value_in: bfloat16 [2048, 8192], P('tp', 'ctx'), may hold values from -6 to 6
- short_weights: float32 [3, 2048, 7], P(None, 'tp'), may hold values from -3 to 3
- filters: float32 [4, 512, 8192], P('tp', 'ctx'), may hold values from 0 to 1
- out_weight: bfloat16 [4096, 2048], P(None, 'tp'), may hold values from -0.125 to 0.125
- cotangent: bfloat16 [4096, 8192], P('tp', 'ctx'), may hold values from -16 to 16
Outputs:
- mixed_out: bfloat16 [4096, 8192], P('tp', 'ctx')
- grad_query: bfloat16 [2048, 8192], P('tp', 'ctx')
- grad_key: bfloat16 [2048, 8192], P('tp', 'ctx')
- grad_value: bfloat16 [2048, 8192], P('tp', 'ctx')
- grad_filters: float32 [4, 512, 8192], P('tp', 'ctx')
- grad_out_weight: float32 [4096, 2048], P('ctx', 'tp')
All inputs are finite; a program needn't handle non-finite values.
Results may differ from a plain program's by a relative error of at most 0.012.
Values may be sent and summed in bfloat16 or wider, within the bound.
No kernel may reach another device: no remote copies, remote signals or barrier semaphores. Data moves between devices by JAX's collectives and lax.ppermute only.
A program may use at most 128 MiB of HBM per device.

v0:
```python
import math
import jax
import jax.numpy as jnp
from jax import lax
from jax.sharding import PartitionSpec as P

BLOCK = 128
TWO_PI = 2.0 * math.pi
HIGHEST = lax.Precision.HIGHEST


def from_behind(value, axis, steps):
    count = lax.axis_size(axis)
    first, last = (max(0, -steps), min(count, count - steps))
    return lax.ppermute(value, axis, [(source, source + steps) for source in range(first, last)])


def fourier_table(count):
    element_indices = jnp.arange(count, dtype=jnp.int32)
    angles = (element_indices[:, None] * element_indices[None, :] % count).astype(jnp.float32) * (
        TWO_PI / count
    )
    return (jnp.cos(angles), -jnp.sin(angles))


def make_tables(length, block_width):
    row_count = 2 * length // block_width
    full_len = row_count * block_width
    outer_re, outer_im = fourier_table(row_count)
    inner_re, inner_im = fourier_table(block_width)
    row_index = jnp.arange(row_count, dtype=jnp.int32)[:, None]
    col_index = jnp.arange(block_width, dtype=jnp.int32)[None, :]
    angles = (row_index * col_index % full_len).astype(jnp.float32) * (TWO_PI / full_len)
    return (outer_re, outer_im, inner_re, inner_im, jnp.cos(angles), -jnp.sin(angles))


def spectrum(signal, tables):
    outer_re, outer_im, inner_re, inner_im, twist_re, twist_im = tables
    channels, length = signal.shape
    block_width = inner_re.shape[0]
    half_rows = length // block_width
    blocks = signal.reshape(channels, half_rows, block_width)
    section_re = jnp.einsum("kn,cnm->ckm", outer_re[:, :half_rows], blocks, precision=HIGHEST)
    section_im = jnp.einsum("kn,cnm->ckm", outer_im[:, :half_rows], blocks, precision=HIGHEST)
    turned_re = section_re * twist_re - section_im * twist_im
    turned_im = section_re * twist_im + section_im * twist_re
    frequency_real_component = jnp.matmul(turned_re, inner_re, precision=HIGHEST) - jnp.matmul(
        turned_im, inner_im, precision=HIGHEST
    )
    spec_im = jnp.matmul(turned_re, inner_im, precision=HIGHEST) + jnp.matmul(
        turned_im, inner_re, precision=HIGHEST
    )
    return (frequency_real_component, spec_im)


def inverse(frequency_real_component, spec_im, tables):
    outer_re, outer_im, inner_re, inner_im, twist_re, twist_im = tables
    channels, row_count, block_width = frequency_real_component.shape
    half_rows = row_count // 2
    back_re = jnp.matmul(frequency_real_component, inner_re, precision=HIGHEST) + jnp.matmul(
        spec_im, inner_im, precision=HIGHEST
    )
    back_im = jnp.matmul(spec_im, inner_re, precision=HIGHEST) - jnp.matmul(
        frequency_real_component, inner_im, precision=HIGHEST
    )
    turned_re = back_re * twist_re + back_im * twist_im
    turned_im = back_im * twist_re - back_re * twist_im
    signal = jnp.einsum("nk,ckm->cnm", outer_re[:half_rows], turned_re, precision=HIGHEST)
    signal = signal + jnp.einsum("nk,ckm->cnm", outer_im[:half_rows], turned_im, precision=HIGHEST)
    return (signal / (row_count * block_width)).reshape(channels, half_rows * block_width)


def causal_taps(stacked, earlier, weights):
    tap_count = weights.shape[2]
    length = stacked.shape[2]
    extended = jnp.concatenate([earlier, stacked], axis=2).astype(jnp.float32)
    running_total = jnp.zeros(stacked.shape, jnp.float32)
    for offset in range(tap_count):
        begin = tap_count - 1 - offset
        running_total = (
            running_total
            + weights[:, :, offset : offset + 1] * extended[:, :, begin : begin + length]
        )
    return running_total


def anticausal_taps(stacked, following, weights):
    tap_count = weights.shape[2]
    length = stacked.shape[2]
    extended = jnp.concatenate([stacked, following], axis=2).astype(jnp.float32)
    running_total = jnp.zeros(stacked.shape, jnp.float32)
    for offset in range(tap_count):
        running_total = (
            running_total
            + weights[:, :, offset : offset + 1] * extended[:, :, offset : offset + length]
        )
    return running_total


def to_channels(block):
    return lax.all_to_all(block, "ctx", split_axis=0, concat_axis=1, tiled=True)


def to_positions(block):
    return lax.all_to_all(block, "ctx", split_axis=1, concat_axis=0, tiled=True)


def per_device(query_in, key_in, value_in, short_weights, filters, out_weight, cotangent):
    tap_count = short_weights.shape[2]
    local_len = query_in.shape[1]
    stacked = jnp.stack([query_in, key_in, value_in])
    earlier = from_behind(stacked[:, :, local_len - (tap_count - 1) :], "ctx", 1)
    shorts = causal_taps(stacked, earlier, short_weights).astype(jnp.bfloat16)
    product = (shorts[1].astype(jnp.float32) * shorts[2].astype(jnp.float32)).astype(jnp.bfloat16)
    product_chan = to_channels(product)
    tables = make_tables(product_chan.shape[1], BLOCK)
    kernel_re, kernel_im = spectrum(filters[0], tables)
    product_re, product_im = spectrum(product_chan.astype(jnp.float32), tables)
    convolved_chan = inverse(
        product_re * kernel_re - product_im * kernel_im,
        product_re * kernel_im + product_im * kernel_re,
        tables,
    ).astype(jnp.bfloat16)
    convolved = to_positions(convolved_chan)
    gated_out = (shorts[0].astype(jnp.float32) * convolved.astype(jnp.float32)).astype(jnp.bfloat16)
    mixed_out = lax.psum_scatter(
        jnp.dot(out_weight, gated_out, preferred_element_type=jnp.float32).astype(jnp.bfloat16),
        "tp",
        scatter_dimension=0,
        tiled=True,
    )
    full_cotangent = lax.all_gather(cotangent, "tp", axis=0, tiled=True)
    grad_gated = lax.dot_general(
        out_weight, full_cotangent, (((0,), (0,)), ((), ())), preferred_element_type=jnp.float32
    )
    grad_out_weight = lax.psum_scatter(
        lax.dot_general(
            full_cotangent, gated_out, (((1,), (1,)), ((), ())), preferred_element_type=jnp.float32
        ),
        "ctx",
        scatter_dimension=0,
        tiled=True,
    )
    grad_conv = (grad_gated * shorts[0].astype(jnp.float32)).astype(jnp.bfloat16)
    grad_chan = to_channels(grad_conv)
    gradient_re, gradient_im = spectrum(grad_chan.astype(jnp.float32), tables)
    grad_product_chan = inverse(
        kernel_re * gradient_re + kernel_im * gradient_im,
        kernel_re * gradient_im - kernel_im * gradient_re,
        tables,
    ).astype(jnp.bfloat16)
    grad_filters = inverse(
        product_re * gradient_re + product_im * gradient_im,
        product_re * gradient_im - product_im * gradient_re,
        tables,
    ).reshape(filters.shape)
    derivative_of_multiple = to_positions(grad_product_chan)
    grad_shorts = jnp.stack(
        [
            grad_gated * convolved.astype(jnp.float32),
            derivative_of_multiple.astype(jnp.float32) * shorts[2].astype(jnp.float32),
            derivative_of_multiple.astype(jnp.float32) * shorts[1].astype(jnp.float32),
        ]
    ).astype(jnp.bfloat16)
    following = from_behind(grad_shorts[:, :, : tap_count - 1], "ctx", -1)
    gradients = anticausal_taps(grad_shorts, following, short_weights).astype(jnp.bfloat16)
    return (mixed_out, gradients[0], gradients[1], gradients[2], grad_filters, grad_out_weight)


def solution(mesh):
    placed = (
        P("tp", "ctx"),
        P("tp", "ctx"),
        P("tp", "ctx"),
        P(None, "tp", None),
        P("tp", "ctx", None),
        P(None, "tp"),
        P("tp", "ctx"),
    )
    return jax.shard_map(
        per_device,
        mesh=mesh,
        in_specs=placed,
        out_specs=(
            P("tp", "ctx"),
            P("tp", "ctx"),
            P("tp", "ctx"),
            P("tp", "ctx"),
            P("tp", "ctx", None),
            P("ctx", "tp"),
        ),
        check_vma=False,
    )
```

profile of v0, /device:TPU:0, one launch (start us, length us, event | category | flops | bytes accessed | tf_op | source)
XLA Modules:
  0.0 518.8 jit_solution(1460974614563037735)
XLA Ops:
  7.2 0.7 all-gather.2.cloned.1.call-update
  7.9 1.0 copy.160
  8.9 1.0 copy.161
  10.0 1.0 copy.162
  11.0 1.7 collective-permute-start
  13.7 0.6 fusion.67
  14.3 0.6 fusion.69
  15.0 0.8 fusion.25
  15.8 0.8 fusion.27
  16.7 1.6 convolution_add_fusion.4
  19.0 0.7 fusion.17
  19.7 0.8 copy.163
  20.5 14.5 %all-to-all-start = ((bf16[64,8,128]{2,1,0:T(8,128)(2,1)}), bf16[64,8,128]{2,1,0:T(8,128)(2,1)}, u32[]{:S(2)}, u32[]{:S(2)}) async-start(bf16[64,8,128]{2,1,0:T(8,128)(2,1)} %bitcast.4), calls=%async_computation | async-start | bytes 262144 | tf_op jit(solution)/shard_map/all_to_all | solution.py:101
  35.0 1.6 convolution_subtract_fusion.4
  36.7 10.6 %all-to-all-done = bf16[64,8,128]{2,1,0:T(8,128)(2,1)} async-done(((bf16[64,8,128]{2,1,0:T(8,128)(2,1)}), bf16[64,8,128]{2,1,0:T(8,128)(2,1)}, u32[]{:S(2)}, u32[]{:S(2)}) %all-to-all-start) | async-done | bytes 131104 | tf_op jit(solution)/shard_map/all_to_all | solution.py:101
  47.3 1.3 convolution_bitcast_fusion.3
  48.6 1.3 convolution_bitcast_fusion.4
  50.0 1.2 fusion.81
  51.2 2.0 convolution_subtract_fusion.5
  53.2 4.0 fusion.54
  57.2 0.8 copy.196
  57.9 4.6 all-to-all-start.2
  63.1 2.0 fusion.80
  65.1 9.9 %all-to-all-done.2 = bf16[64,8,128]{2,1,0:T(8,128)(2,1)S(1)} async-done(((bf16[64,8,128]{2,1,0:T(8,128)(2,1)}), bf16[64,8,128]{2,1,0:T(8,128)(2,1)S(1)}, u32[]{:S(2)}, u32[]{:S(2)}) %all-to-all-start.2) | async-done | bytes 131104 | tf_op jit(solution)/shard_map/all_to_all | solution.py:101
  75.9 1.2 fusion.82
  77.1 1.2 fusion.83
  78.3 1.2 convolution_add_fusion.2
  79.6 1.2 convolution_subtract_fusion.2
  80.8 1.4 multiply_add_fusion
  82.2 0.9 fusion.110
  83.1 0.9 fusion.112
  84.0 0.9 convolution_subtract_fusion.3
  84.9 0.9 convolution_add_fusion.3
  85.8 0.9 fusion.46
  86.7 0.8 fusion.8
  87.6 16.5 %all_to_all.49 = bf16[8,64,128]{2,0,1:T(8,128)(2,1)S(1)} all-to-all(bf16[8,64,128]{2,0,1:T(8,128)(2,1)S(1)} %copy.193), channel_id=1, replica_groups=mesh['ctx'=64,'tp'=4] {'ctx'}, dimensions={1} | all-to-all | bytes 262144 | tf_op jit(solution)/shard_map/all_to_all | solution.py:105
  104.3 4.7 fusion
  109.1 5.8 %convolution_bitcast_fusion = f32[4096,512]{0,1:T(8,128)} fusion(bf16[4096,128]{1,0:T(8,128)(2,1)} %all-gather.2.cloned.1.call-done, f32[512,128]{0,1:T(8,128)S(1)} %copy.194, bf16[3,512,128]{1,2,0:T(8,128)(2,1)S(1)} %copy-done.4), kind=kOutput, calls=%fused_computation | convolution fusion | flops 537067520 | bytes 9830400 | tf_op jit(solution)/shard_map/dot_general | solution.py:137
  114.9 9.1 %copy.324 = f32[4096,512]{1,0:T(8,128)} copy(f32[4096,512]{0,1:T(8,128)} %convolution_bitcast_fusion) | data formatting | bytes 16777216
  124.0 0.9 fusion.104
  124.9 0.9 fusion.106
  125.8 0.9 convolution_subtract_fusion.1
  126.7 0.9 convolution_add_fusion.1
  127.6 0.8 fusion.39
  128.3 0.8 fusion.7
  129.1 0.7 copy.218
  129.8 4.8 all-to-all-start.3
  134.7 0.9 fusion.102
  135.6 0.9 fusion.100
  136.5 0.9 convolution_add_fusion
  137.4 0.9 convolution_subtract_fusion
  138.3 0.8 fusion.32
  139.1 8.1 %all-to-all-done.3 = bf16[8,64,128]{2,0,1:T(8,128)(2,1)S(1)} async-done(((bf16[8,64,128]{2,0,1:T(8,128)(2,1)}), bf16[8,64,128]{2,0,1:T(8,128)(2,1)S(1)}, u32[]{:S(2)}, u32[]{:S(2)}) %all-to-all-start.3) | async-done | bytes 131104 | tf_op jit(solution)/shard_map/all_to_all | solution.py:105
  147.4 1.0 fusion.71
  148.4 1.3 collective-permute-start.1
  149.7 0.8 fusion.2
  150.4 0.8 reshape_reshape.3
  151.2 3.0 collective-permute-done.1
  154.4 0.7 fusion.10
  155.1 0.8 copy.236
  155.8 0.8 copy.235
  156.6 0.8 copy.234
  157.3 1.8 copy.233
  159.1 352.9 %reduce-scatter.7.cloned.1.call-done = f32[64,512]{1,0:T(8,128)} async-done(((f32[4096,512]{1,0:T(8,128)}), f32[64,512]{1,0:T(8,128)}) %reduce-scatter.7.cloned.1.call-update) | async-done | bytes 131088
  (80 shorter events, 3.8 us)
Async XLA Ops:
  7.2 6.6 %copy-start = (f32[1,8,8192]{2,1,0:T(8,128)S(1)}, f32[1,8,8192]{2,1,0:T(8,128)}, u32[]{:S(2)}) copy-start(f32[1,8,8192]{2,1,0:T(8,128)} %param.11) | copy-start | bytes 786436
  7.2 9.5 %copy-start.23 = (f32[3,512,7]{1,2,0:T(8,128)S(1)}, f32[3,512,7]{1,2,0:T(8,128)}, u32[]{:S(2)}) copy-start(f32[3,512,7]{1,2,0:T(8,128)} %param.10) | copy-start | bytes 129028
  7.2 46.0 %all-gather.2.cloned.1.call-start = ((), (), s32[]{:S(2)}) async-start(), calls=%async_computation.7 | async-start | bytes 1310720 | tf_op jit(solution)/shard_map/all_gather | solution.py:132
  11.0 7.4 %collective-permute-start = (bf16[3,512,6]{1,2,0:T(8,128)(2,1)S(1)}, bf16[3,512,6]{1,2,0:T(8,128)(2,1)S(1)}, u32[]{:S(2)}, u32[]{:S(2)}) collective-permute-start(bf16[3,512,6]{1,2,0:T(8,128)(2,1)S(1)} %pad_maximum_fusion.2), channel_id=1, source_target_pairs={{0,4},{4,8},{8,12},{12,16},{16,20},{20,24},{24,28},{28,32},{32,36}... | collective-permute-start | bytes 55304 | tf_op jit(solution)/shard_map/ppermute | solution.py:15
  12.9 62.5 %copy-start.11 = (f32[128,128]{0,1:T(8,128)}, f32[128,128]{0,1:T(8,128)S(1)}, u32[]{:S(2)}) copy-start(f32[128,128]{0,1:T(8,128)S(1)} %fusion.126) | copy-start | bytes 196612
  13.2 61.8 %copy-start.9 = (f32[128,128]{0,1:T(8,128)}, f32[128,128]{0,1:T(8,128)S(1)}, u32[]{:S(2)}) copy-start(f32[128,128]{0,1:T(8,128)S(1)} %sine_negate_fusion.1) | copy-start | bytes 196612
  18.3 0.6 copy-start.13
  18.3 0.6 copy-start.15
  18.4 0.6 copy-start.17
  18.4 0.6 copy-start.19
  18.4 0.6 copy-start.21
  19.7 33.5 %copy-start.3 = (bf16[3,512,128]{1,2,0:T(8,128)(2,1)}, bf16[3,512,128]{1,2,0:T(8,128)(2,1)S(1)}, u32[]{:S(2)}) copy-start(bf16[3,512,128]{1,2,0:T(8,128)(2,1)S(1)} %fusion.17) | copy-start | bytes 1179652
  20.5 26.8 %all-to-all-start = ((bf16[64,8,128]{2,1,0:T(8,128)(2,1)}), bf16[64,8,128]{2,1,0:T(8,128)(2,1)}, u32[]{:S(2)}, u32[]{:S(2)}) async-start(bf16[64,8,128]{2,1,0:T(8,128)(2,1)} %bitcast.4), calls=%async_computation | async-start | bytes 262144 | tf_op jit(solution)/shard_map/all_to_all | solution.py:101
  57.9 17.0 %all-to-all-start.2 = ((bf16[64,8,128]{2,1,0:T(8,128)(2,1)}), bf16[64,8,128]{2,1,0:T(8,128)(2,1)S(1)}, u32[]{:S(2)}, u32[]{:S(2)}) async-start(bf16[64,8,128]{2,1,0:T(8,128)(2,1)} %bitcast.34), calls=%async_computation.3 | async-start | bytes 262144 | tf_op jit(solution)/shard_map/all_to_all | solution.py:101
  62.6 94.8 %reduce-scatter.5.cloned.1.call-start = ((), (), s32[]{:S(2)}) async-start(), calls=%async_computation.6 | async-start | bytes 1310720 | tf_op jit(solution)/shard_map/reduce_scatter | solution.py:126
  75.4 5.4 %copy-start.5 = (f32[8,128,128]{2,1,0:T(8,128)S(1)}, f32[8,128,128]{2,1,0:T(8,128)}, u32[]{:S(2)}) copy-start(f32[8,128,128]{2,1,0:T(8,128)} %convolution_add_fusion.4) | copy-start | bytes 1572868
  75.4 5.4 %copy-start.6 = (f32[8,128,128]{2,1,0:T(8,128)S(1)}, f32[8,128,128]{2,1,0:T(8,128)}, u32[]{:S(2)}) copy-start(f32[8,128,128]{2,1,0:T(8,128)} %convolution_subtract_fusion.4) | copy-start | bytes 1572868
  75.5 5.4 %copy-start.7 = (f32[8,128,128]{2,1,0:T(8,128)S(1)}, f32[8,128,128]{2,1,0:T(8,128)}, u32[]{:S(2)}) copy-start(f32[8,128,128]{2,1,0:T(8,128)} %convolution_subtract_fusion.5) | copy-start | bytes 1572868
  75.5 5.4 %copy-start.8 = (f32[8,128,128]{2,1,0:T(8,128)S(1)}, f32[8,128,128]{2,1,0:T(8,128)}, u32[]{:S(2)}) copy-start(f32[8,128,128]{2,1,0:T(8,128)} %fusion.80) | copy-start | bytes 1572868
  82.2 3.6 copy-start.12
  82.2 4.5 copy-start.10
  83.1 21.1 %copy-start.4 = (bf16[3,512,128]{1,2,0:T(8,128)(2,1)S(1)}, bf16[3,512,128]{1,2,0:T(8,128)(2,1)}, u32[]{:S(2)}) copy-start(bf16[3,512,128]{1,2,0:T(8,128)(2,1)} %copy-done.3) | copy-start | bytes 1179652
  104.2 10.6 %copy-start.1 = (f32[512,128]{0,1:T(8,128)}, f32[512,128]{0,1:T(8,128)S(1)}, u32[]{:S(2)}) copy-start(f32[512,128]{0,1:T(8,128)S(1)} %copy.194) | copy-start | bytes 786436
  109.0 403.0 %reduce-scatter.7.cloned.1.call-start = ((), (), s32[]{:S(2)}) async-start(), calls=%async_computation.8 | async-start | bytes 8519680
  129.8 17.3 %all-to-all-start.3 = ((bf16[8,64,128]{2,0,1:T(8,128)(2,1)}), bf16[8,64,128]{2,0,1:T(8,128)(2,1)S(1)}, u32[]{:S(2)}, u32[]{:S(2)}) async-start(bf16[8,64,128]{2,0,1:T(8,128)(2,1)} %copy.218), calls=%async_computation.4 | async-start | bytes 262144 | tf_op jit(solution)/shard_map/all_to_all | solution.py:105
  134.7 12.7 %copy-start.2 = (f32[512,128]{0,1:T(8,128)S(1)}, f32[512,128]{0,1:T(8,128)}, u32[]{:S(2)}) copy-start(f32[512,128]{0,1:T(8,128)} %copy-done.1) | copy-start | bytes 786436
  138.3 16.0 %copy-start.14 = (f32[3,512]{1,0:T(4,128)S(1)}, f32[3,512]{1,0:T(4,128)}, u32[]{:S(2)}) copy-start(f32[3,512]{1,0:T(4,128)} %copy-done.13) | copy-start | bytes 18436
  138.3 16.0 %copy-start.16 = (f32[3,512]{1,0:T(4,128)S(1)}, f32[3,512]{1,0:T(4,128)}, u32[]{:S(2)}) copy-start(f32[3,512]{1,0:T(4,128)} %copy-done.15) | copy-start | bytes 18436
  138.3 16.0 %copy-start.18 = (f32[3,512]{1,0:T(4,128)S(1)}, f32[3,512]{1,0:T(4,128)}, u32[]{:S(2)}) copy-start(f32[3,512]{1,0:T(4,128)} %copy-done.17) | copy-start | bytes 18436
  138.3 16.0 %copy-start.20 = (f32[3,512]{1,0:T(4,128)S(1)}, f32[3,512]{1,0:T(4,128)}, u32[]{:S(2)}) copy-start(f32[3,512]{1,0:T(4,128)} %copy-done.19) | copy-start | bytes 18436
  138.3 16.0 %copy-start.22 = (f32[3,512,1]{1,0,2:T(4,128)S(1)}, f32[3,512,1]{1,0,2:T(4,128)}, u32[]{:S(2)}) copy-start(f32[3,512,1]{1,0,2:T(4,128)} %copy-done.21) | copy-start | bytes 18436
  148.4 5.9 %collective-permute-start.1 = (bf16[3,512,6]{1,2,0:T(8,128)(2,1)S(1)}, bf16[3,512,6]{1,2,0:T(8,128)(2,1)S(1)}, u32[]{:S(2)}, u32[]{:S(2)}) collective-permute-start(bf16[3,512,6]{1,2,0:T(8,128)(2,1)S(1)} %pad_maximum_fusion), channel_id=1, source_target_pairs={{4,0},{8,4},{12,8},{16,12},{20,16},{24,20},{28,24},{32,28},{36,32}... | collective-permute-start | bytes 55304 | tf_op jit(solution)/shard_map/ppermute | solution.py:15
Sparse Core Ops, SparseCore 0:
  9.8 24.0 all-gather.1
  109.1 15.6 reduce-scatter.4
  127.9 384.0 reduce-scatter.6
where the time goes:
time: 528 us; the launch traced here: 519 us
  waiting for transfers between devices  385 us (73%)
  matrix products  51 us (10%)
  starting transfers between devices  27.6 us (5%)
  local copies, waits for them, and re-layouts  20.4 us (4%)
  blocking collectives  16.5 us (3%)
  between operations  14.7 us (3%)
    unnamed x4, waiting for transfers between devices  354 us
    all_to_all x2, waiting for transfers between devices, to_channels(): return lax.all_to_all(block, 'ctx', split_axis=0, concat_axis=1, tiled=True)  20.5 us
    all_to_all x2, starting transfers between devices, to_channels(): return lax.all_to_all(block, 'ctx', split_axis=0, concat_axis=1, tiled=True)  19.2 us
    unnamed x60, local copies, waits for them, and re-layouts  16.8 us
    all_to_all x1, blocking collectives, to_positions(): return lax.all_to_all(block, 'ctx', split_axis=1, concat_axis=0, tiled=True)  16.5 us
  transfers between devices with their start and end apart: 8, of which 5 were waited for; matrix products, arithmetic and copies ran while one was open for 10% of the time, Pallas kernels for 0%

commit v1 on v0

--- a/solution.py
+++ b/solution.py
@@ -98,7 +98,10 @@
 
 
 def to_channels(block):
-    return lax.all_to_all(block, "ctx", split_axis=0, concat_axis=1, tiled=True)
+    return jnp.concatenate(
+        lax.all_to_all(jnp.stack(jnp.split(block, lax.axis_size("ctx"), axis=0)), "ctx", 0, 0),
+        axis=1,
+    )
 
 
 def to_positions(block):

time: 528 us -> 602 us (1.14)
  local copies, waits for them, and re-layouts: 20.4 us -> 89.2 us
    unnamed x60 -> x190, local copies, waits for them, and re-layouts: 16.8 us -> 85.5 us
    ppermute x2, waiting for transfers between devices: 3.04 us -> 11.5 us  [from_behind(): lax.ppermute(value, axis, [(source, source + steps) for source in range(f...]
    unnamed x4, waiting for transfers between devices: 354 us -> 346 us
  transfers between devices with their start and end apart: 8 -> 8, of which waited for: 5 -> 6; matrix products, arithmetic and copies ran while one was open for 10% -> 15% of each run, Pallas kernels for 0% -> 0%
where the time goes in v1:
time: 602 us; the launch traced here: 595 us
  waiting for transfers between devices  387 us (64%)
  local copies, waits for them, and re-layouts  89.2 us (15%)
  matrix products  47.1 us (8%)
  starting transfers between devices  30.9 us (5%)
  blocking collectives  16.5 us (3%)
  between operations  14.8 us (2%)
  other arithmetic  9.43 us (2%)
    unnamed x4, waiting for transfers between devices  346 us
    unnamed x190, local copies, waits for them, and re-layouts  85.5 us
    all_to_all x2, starting transfers between devices, to_channels(): lax.all_to_all(jnp.stack(jnp.split(block, lax.axis_size('ctx'), axis=0)),...  21.9 us
    all_to_all x2, waiting for transfers between devices, to_channels(): lax.all_to_all(jnp.stack(jnp.split(block, lax.axis_size('ctx'), axis=0)),...  21 us
    all_to_all x1, blocking collectives, to_positions(): return lax.all_to_all(block, 'ctx', split_axis=1, concat_axis=0, tiled=True)  16.5 us
  transfers between devices with their start and end apart: 8, of which 6 were waited for; matrix products, arithmetic and copies ran while one was open for 15% of the time, Pallas kernels for 0%

profile of v1, /device:TPU:0, one launch (start us, length us, event | category | flops | bytes accessed | tf_op | source)
XLA Modules:
  0.0 594.6 jit_solution(15430812176391054087)
XLA Ops:
  7.2 0.7 all-gather.2.cloned.1.call-update
  7.9 1.2 pad_maximum_fusion.2
  9.1 1.7 collective-permute-start
  11.9 0.6 fusion.68
  12.5 0.6 fusion.70
  13.2 0.8 fusion.25
  14.0 0.8 fusion.27
  14.9 1.6 convolution_add_fusion.4
  16.6 2.5 collective-permute-done
  19.5 3.0 fusion.17
  22.6 0.6 constant_dynamic-update-slice_fusion.63
  31.8 0.6 constant_dynamic-update-slice_fusion.47
  42.8 0.6 constant_dynamic-update-slice_fusion.28
  53.8 0.6 constant_dynamic-update-slice_fusion.9
  59.6 17.3 %all-to-all-start = ((bf16[64,8,128]{2,1,0:T(8,128)(2,1)}), bf16[64,8,128]{2,1,0:T(8,128)(2,1)S(1)}, u32[]{:S(2)}, u32[]{:S(2)}) async-start(bf16[64,8,128]{2,1,0:T(8,128)(2,1)} %constant_dynamic-update-slice_fusion), calls=%async_computation | async-start | bytes 262144 | tf_op jit(solution)/shard_map/all_to_all | solution.py:102
  76.9 1.6 convolution_subtract_fusion.4
  78.6 10.8 %all-to-all-done = bf16[64,8,128]{2,1,0:T(8,128)(2,1)S(1)} async-done(((bf16[64,8,128]{2,1,0:T(8,128)(2,1)}), bf16[64,8,128]{2,1,0:T(8,128)(2,1)S(1)}, u32[]{:S(2)}, u32[]{:S(2)}) %all-to-all-start) | async-done | bytes 131104 | tf_op jit(solution)/shard_map/all_to_all | solution.py:102
  90.3 1.2 fusion.80
  91.5 2.0 convolution_subtract_fusion.5
  93.5 4.5 fusion.54
  100.3 0.6 constant_dynamic-update-slice_fusion.123
  111.3 0.6 constant_dynamic-update-slice_fusion.104
  135.0 4.6 all-to-all-start.2
  139.9 2.0 fusion.79
  141.9 10.2 %all-to-all-done.2 = bf16[64,8,128]{2,1,0:T(8,128)(2,1)S(1)} async-done(((bf16[64,8,128]{2,1,0:T(8,128)(2,1)}), bf16[64,8,128]{2,1,0:T(8,128)(2,1)S(1)}, u32[]{:S(2)}, u32[]{:S(2)}) %all-to-all-start.2) | async-done | bytes 131104 | tf_op jit(solution)/shard_map/all_to_all | solution.py:102
  153.0 1.2 fusion.81
  154.2 1.2 fusion.82
  155.4 1.2 convolution_add_fusion.2
  156.6 1.2 convolution_subtract_fusion.2
  158.1 2.2 multiply_add_fusion
  160.3 0.9 fusion.109
  161.2 0.9 fusion.111
  162.1 0.9 convolution_subtract_fusion.3
  163.0 0.9 convolution_add_fusion.3
  163.9 0.9 fusion.46
  164.8 0.8 fusion.8
  165.7 16.5 %all_to_all.30 = bf16[8,64,128]{2,0,1:T(8,128)(2,1)S(1)} all-to-all(bf16[8,64,128]{2,0,1:T(8,128)(2,1)S(1)} %copy.266), channel_id=1, replica_groups=mesh['ctx'=64,'tp'=4] {'ctx'}, dimensions={1} | all-to-all | bytes 262144 | tf_op jit(solution)/shard_map/all_to_all | solution.py:108
  182.2 2.5 fusion
  184.8 1.1 copy-done.3
  185.9 4.5 convolution_bitcast_fusion
  190.4 9.1 %copy.390 = f32[4096,512]{1,0:T(8,128)} copy(f32[4096,512]{0,1:T(8,128)} %convolution_bitcast_fusion) | data formatting | bytes 16777216
  199.5 0.9 fusion.103
  200.6 0.9 fusion.105
  201.5 0.9 convolution_subtract_fusion.1
  202.4 0.9 convolution_add_fusion.1
  203.3 0.8 fusion.39
  204.1 0.8 fusion.7
  204.9 0.7 copy.289
  205.6 5.7 all-to-all-start.3
  211.3 0.9 fusion.101
  212.2 0.9 fusion.99
  213.1 0.9 convolution_add_fusion
  214.0 0.9 convolution_subtract_fusion
  214.9 0.8 fusion.32
  215.7 7.8 %all-to-all-done.3 = bf16[8,64,128]{2,0,1:T(8,128)(2,1)} async-done(((bf16[8,64,128]{2,0,1:T(8,128)(2,1)}), bf16[8,64,128]{2,0,1:T(8,128)(2,1)}, u32[]{:S(2)}, u32[]{:S(2)}) %all-to-all-start.3) | async-done | bytes 131104 | tf_op jit(solution)/shard_map/all_to_all | solution.py:108
  223.5 1.0 fusion.52
  224.6 1.3 collective-permute-start.1
  225.9 0.8 fusion.2
  226.7 0.8 reshape_reshape.3
  227.5 8.9 %collective-permute-done.1 = bf16[3,512,6]{2,1,0:T(8,128)(2,1)S(1)} collective-permute-done((bf16[3,512,6]{2,1,0:T(8,128)(2,1)S(1)}, bf16[3,512,6]{2,1,0:T(8,128)(2,1)S(1)}, u32[]{:S(2)}, u32[]{:S(2)}) %collective-permute-start.1) | collective-permute-done | bytes 18464 | tf_op jit(solution)/shard_map/ppermute | solution.py:15
  236.6 3.0 fusion.10
  239.6 0.8 slice_bitcast_fusion
  240.3 1.8 copy.302
  242.1 345.7 %reduce-scatter.7.cloned.1.call-done = f32[64,512]{1,0:T(8,128)} async-done(((f32[4096,512]{1,0:T(8,128)}), f32[64,512]{1,0:T(8,128)}) %reduce-scatter.7.cloned.1.call-update) | async-done | bytes 131088
  (206 shorter events, 74.9 us)
Async XLA Ops:
  7.2 4.7 copy-start
  7.2 86.3 %all-gather.2.cloned.1.call-start = ((), (), s32[]{:S(2)}) async-start(), calls=%async_computation.7 | async-start | bytes 1310720 | tf_op jit(solution)/shard_map/all_gather | solution.py:135
  9.1 10.1 %collective-permute-start = (bf16[3,512,6]{2,1,0:T(8,128)(2,1)S(1)}, bf16[3,512,6]{2,1,0:T(8,128)(2,1)S(1)}, u32[]{:S(2)}, u32[]{:S(2)}) collective-permute-start(bf16[3,512,6]{2,1,0:T(8,128)(2,1)S(1)} %pad_maximum_fusion.2), channel_id=1, source_target_pairs={{0,4},{4,8},{8,12},{12,16},{16,20},{20,24},{24,28},{28,32},{32,36}... | collective-permute-start | bytes 55304 | tf_op jit(solution)/shard_map/ppermute | solution.py:15
  11.1 152.8 %copy-start.11 = (f32[128,128]{0,1:T(8,128)}, f32[128,128]{0,1:T(8,128)S(1)}, u32[]{:S(2)}) copy-start(f32[128,128]{0,1:T(8,128)S(1)} %fusion.127) | copy-start | bytes 196612
  11.4 153.5 %copy-start.8 = (f32[128,128]{0,1:T(8,128)}, f32[128,128]{0,1:T(8,128)S(1)}, u32[]{:S(2)}) copy-start(f32[128,128]{0,1:T(8,128)S(1)} %sine_negate_fusion.1) | copy-start | bytes 196612
  13.1 1.7 copy-start.28
  14.8 4.3 copy-start.15
  14.8 4.3 copy-start.16
  14.9 4.3 copy-start.17
  16.6 5.9 copy-start.18
  16.6 5.9 copy-start.20
  16.6 5.9 copy-start.22
  16.6 5.9 copy-start.24
  16.6 5.9 copy-start.26
  59.6 29.7 %all-to-all-start = ((bf16[64,8,128]{2,1,0:T(8,128)(2,1)}), bf16[64,8,128]{2,1,0:T(8,128)(2,1)S(1)}, u32[]{:S(2)}, u32[]{:S(2)}) async-start(bf16[64,8,128]{2,1,0:T(8,128)(2,1)} %constant_dynamic-update-slice_fusion), calls=%async_computation | async-start | bytes 262144 | tf_op jit(solution)/shard_map/all_to_all | solution.py:102
  135.0 17.0 %all-to-all-start.2 = ((bf16[64,8,128]{2,1,0:T(8,128)(2,1)}), bf16[64,8,128]{2,1,0:T(8,128)(2,1)S(1)}, u32[]{:S(2)}, u32[]{:S(2)}) async-start(bf16[64,8,128]{2,1,0:T(8,128)(2,1)} %constant_dynamic-update-slice_fusion.64), calls=%async_computation.3 | async-start | bytes 262144 | tf_op jit(solution)/shard_map/all_to_all | solution.py:102
  139.6 100.7 %reduce-scatter.5.cloned.1.call-start = ((), (), s32[]{:S(2)}) async-start(), calls=%async_computation.6 | async-start | bytes 1310720 | tf_op jit(solution)/shard_map/reduce_scatter | solution.py:129
  156.6 1.3 copy-start.4
  156.6 1.3 copy-start.5
  156.6 1.3 copy-start.6
  156.6 1.5 copy-start.7
  163.0 19.2 %copy-start.1 = (bf16[4096,512]{1,0:T(8,128)(2,1)S(1)}, bf16[4096,512]{1,0:T(8,128)(2,1)}, u32[]{:S(2)}) copy-start(bf16[4096,512]{1,0:T(8,128)(2,1)} %param.12) | copy-start | bytes 12582916
  184.7 1.2 copy-start.3
  184.7 403.1 %reduce-scatter.7.cloned.1.call-start = ((), (), s32[]{:S(2)}) async-start(), calls=%async_computation.8 | async-start | bytes 8519680
  199.5 1.0 copy-start.2
  201.5 1.8 copy-start.12
  202.4 1.7 copy-start.9
  205.6 17.9 %all-to-all-start.3 = ((bf16[8,64,128]{2,0,1:T(8,128)(2,1)}), bf16[8,64,128]{2,0,1:T(8,128)(2,1)}, u32[]{:S(2)}, u32[]{:S(2)}) async-start(bf16[8,64,128]{2,0,1:T(8,128)(2,1)} %copy.289), calls=%async_computation.4 | async-start | bytes 262144 | tf_op jit(solution)/shard_map/all_to_all | solution.py:108
  213.1 1.8 copy-start.13
  214.0 10.5 %copy-start.14 = (f32[512,128]{1,0:T(8,128)S(1)}, f32[512,128]{1,0:T(8,128)}, u32[]{:S(2)}) copy-start(f32[512,128]{1,0:T(8,128)} %get-tuple-element.53) | copy-start | bytes 786436
  214.9 11.0 %copy-start.10 = (f32[128,128]{0,1:T(8,128)S(1)}, f32[128,128]{0,1:T(8,128)}, u32[]{:S(2)}) copy-start(f32[128,128]{0,1:T(8,128)} %copy-done.8) | copy-start | bytes 196612
  224.6 11.8 %collective-permute-start.1 = (bf16[3,512,6]{2,1,0:T(8,128)(2,1)S(1)}, bf16[3,512,6]{2,1,0:T(8,128)(2,1)S(1)}, u32[]{:S(2)}, u32[]{:S(2)}) collective-permute-start(bf16[3,512,6]{2,1,0:T(8,128)(2,1)S(1)} %pad_maximum_fusion), channel_id=1, source_target_pairs={{4,0},{8,4},{12,8},{16,12},{20,16},{24,20},{28,24},{32,28},{36,32}... | collective-permute-start | bytes 55304 | tf_op jit(solution)/shard_map/ppermute | solution.py:15
  226.7 9.9 %copy-start.19 = (f32[3,512]{1,0:T(4,128)S(1)}, f32[3,512]{1,0:T(4,128)}, u32[]{:S(2)}) copy-start(f32[3,512]{1,0:T(4,128)} %copy-done.18) | copy-start | bytes 18436
  226.7 9.9 %copy-start.21 = (f32[3,512]{1,0:T(4,128)S(1)}, f32[3,512]{1,0:T(4,128)}, u32[]{:S(2)}) copy-start(f32[3,512]{1,0:T(4,128)} %copy-done.20) | copy-start | bytes 18436
  226.7 9.9 %copy-start.23 = (f32[3,512]{1,0:T(4,128)S(1)}, f32[3,512]{1,0:T(4,128)}, u32[]{:S(2)}) copy-start(f32[3,512]{1,0:T(4,128)} %copy-done.22) | copy-start | bytes 18436
  226.7 9.9 %copy-start.25 = (f32[3,512]{1,0:T(4,128)S(1)}, f32[3,512]{1,0:T(4,128)}, u32[]{:S(2)}) copy-start(f32[3,512]{1,0:T(4,128)} %copy-done.24) | copy-start | bytes 18436
  226.7 9.9 %copy-start.27 = (f32[3,512,1]{1,0,2:T(4,128)S(1)}, f32[3,512,1]{1,0,2:T(4,128)}, u32[]{:S(2)}) copy-start(f32[3,512,1]{1,0,2:T(4,128)} %copy-done.26) | copy-start | bytes 18436
Sparse Core Ops, SparseCore 0:
  9.8 24.1 all-gather.1
  184.8 15.9 reduce-scatter.4
  203.9 383.8 reduce-scatter.6
